TPU v7x, 32 devices: a whole 2x2x4 slice. The times are simulated.
32 devices in a mesh: groups: 2 (over y), tp: 16 (over z, x, core).
Axes of the slice: x: 2, y: 2, z: 4, core: 2. Of those that a mesh axis runs over, the one named last changes fastest.
Arguments:
- hidden_in: bfloat16 [32, 8, 512], P(('groups', 'tp')), parts along dimension 0, may hold values from -6 to 6
- norm_gain: float32 [8192], replicated, may hold values from 0.1 to 1.9
- q_blocks: bfloat16 [16, 16, 128, 2048], P('tp'), may hold values from -0.0625 to 0.0625
- o_blocks: bfloat16 [16, 2048, 16, 128], P('tp'), may hold values from -1.5 to 1.5
- kv_blocks: bfloat16 [2, 1024, 8192], P(None, None, 'tp'), may hold values from -0.0625 to 0.0625
- kv_assign: int32 [16], replicated, may hold values from 0 to 7, as said below
- key_cache: bfloat16 [32, 8, 2048, 128], P(('groups', 'tp')), parts along dimension 0, may hold values from -240 to 240
- value_cache: bfloat16 [32, 8, 2048, 128], P(('groups', 'tp')), parts along dimension 0, may hold values from -6 to 6
- lengths: int32 [32, 8], P(('groups', 'tp')), parts along dimension 0, may hold values from 1 to 2048, as said below
Outputs:
- attn_out: bfloat16 [32, 8, 512], P(('groups', 'tp')), parts along dimension 0
There are 2 independent parts, one for each index of `groups`. A program takes and returns all parts, laid end to end along the dimension named above; an argument that names none is the same for every part. Nothing has to cross between parts.
Inputs may be any that keep to these rules, and one draw needn't show every extreme that they name: `kv_assign`: entries 2m and 2m + 1 are equal, and each of the 8 key-value heads is named by exactly two entries. `lengths`: in every rank one row has all 2048 positions valid.
All inputs are finite; a program needn't handle non-finite values.
Results may differ from a plain program's by a relative error of at most 0.011.
The roundings to bfloat16 on the way count: a program that leaves them out, or rounds other values in their place, can miss the bound.
Values may be sent and summed in bfloat16 or wider, within the bound.
No kernel may reach another device: no remote copies, remote signals or barrier semaphores. Data moves between devices by JAX's collectives and lax.ppermute only.
A program may use at most 128 MiB of HBM per device.

v0:
```python
import jax
import jax.numpy as jnp
from jax import lax
from jax.sharding import PartitionSpec as P

D = 8192
KVH = 8
HD = 128
ROLL = 16
ROWS = 8
GR = 4
QG = 16
DS = 512


def from_partner(value, axis, bit):
    mask = 2**bit
    pairs = [(source, source ^ mask) for source in range(lax.axis_size(axis))]
    return lax.ppermute(value, axis, pairs)


def norm_rows(rows_float, norm_gain):
    mean_square = jnp.mean(rows_float * rows_float, axis=-1, keepdims=True)
    return (rows_float * lax.rsqrt(mean_square + 1e-05) * norm_gain[None, :]).astype(jnp.bfloat16)


def local(
    hidden_in, norm_gain, q_blocks, o_blocks, kv_blocks, kv_assign, key_cache, value_cache, lengths
):
    ranks = lax.axis_size("tp")
    my_index = lax.axis_index("tp")
    my_rank = my_index % ROLL
    my_half = my_rank % 2
    grid_cols = ranks // GR
    group_count = ranks // ROLL
    col_width = q_blocks.shape[3]
    key_width = kv_blocks.shape[2]
    grid_row = my_index // grid_cols
    grid_col = my_index % grid_cols
    dest_ids = jnp.arange(ranks, dtype=jnp.int32)
    dest_rank = dest_ids % ROLL
    dest_head = kv_assign[dest_rank]
    dest_group = 2 * dest_head + dest_rank % 2
    dest_copy = dest_ids // ROLL
    every_rows = lax.all_gather(hidden_in, "tp", axis=0, tiled=True)
    rows_float = (
        every_rows.reshape(group_count, ROLL, ROWS, DS)
        .transpose(0, 2, 1, 3)
        .reshape(group_count * ROWS, D)
        .astype(jnp.float32)
    )
    normed_every = norm_rows(rows_float, norm_gain)
    col_rows = lax.dynamic_slice_in_dim(normed_every, grid_col * col_width, col_width, 1)
    query_part = jnp.einsum(
        "rc,aec->rae", col_rows, q_blocks[0], preferred_element_type=jnp.float32
    )
    query_part = (
        query_part.reshape(group_count, ROWS, QG, HD)
        .transpose(0, 2, 1, 3)
        .reshape(group_count * QG, ROWS, HD)
    )
    query_pick = jnp.take(query_part, dest_copy * QG + dest_group, axis=0)
    slot_mask = (jnp.arange(GR, dtype=jnp.int32) == grid_row).astype(jnp.float32)
    query_term = (query_pick[:, :, None, :] * slot_mask[None, None, :, None]).reshape(
        ranks, ROWS, GR * HD
    )
    key_rows = lax.dynamic_slice_in_dim(normed_every, my_index * key_width, key_width, 1)
    keyval_part = jnp.einsum("rc,kfc->rkf", key_rows, kv_blocks, preferred_element_type=jnp.float32)
    keyval_part = (
        keyval_part.reshape(group_count, ROWS, 2, KVH, HD)
        .transpose(0, 3, 1, 2, 4)
        .reshape(group_count * KVH, ROWS, 2 * HD)
    )
    keyval_term = jnp.take(keyval_part, dest_copy * KVH + dest_head, axis=0)
    proj_term = jnp.concatenate([query_term, keyval_term], -1).reshape(ranks * ROWS, (GR + 2) * HD)
    projected = lax.psum_scatter(proj_term, "tp", scatter_dimension=0, tiled=True)
    queries = projected[:, : GR * HD].astype(jnp.bfloat16)
    keyval_new = projected[:, GR * HD :].astype(jnp.bfloat16)
    key_new = keyval_new[:, :HD]
    value_new = keyval_new[:, HD:]
    partner_queries = from_partner(queries, "tp", 0)
    both_queries = jnp.where(
        my_half == 0,
        jnp.concatenate([queries, partner_queries], 1),
        jnp.concatenate([partner_queries, queries], 1),
    )
    both_queries = both_queries.reshape(ROWS, 2 * GR, HD)
    scale = 1.0 / HD**0.5
    scores = (
        jnp.einsum("bhe,bte->bht", both_queries, key_cache[0], preferred_element_type=jnp.float32)
        * scale
    )
    positions = jnp.arange(scores.shape[2], dtype=jnp.int32)
    masked = positions[None, None, :] < lengths[0][:, None, None]
    new_score = (
        jnp.einsum("bhe,be->bh", both_queries, key_new, preferred_element_type=jnp.float32) * scale
    )
    new_score = jnp.where(my_half == 0, new_score, jnp.float32(-1e30))
    top = jnp.maximum(jnp.max(jnp.where(masked, scores, jnp.float32(-1e30)), axis=-1), new_score)
    weights = jnp.where(masked, jnp.exp(scores - top[..., None]), jnp.float32(0.0))
    new_weight = jnp.exp(new_score - top)
    total = jnp.sum(weights, axis=-1) + new_weight
    summed = jnp.einsum(
        "bht,bte->bhe",
        weights.astype(jnp.bfloat16),
        value_cache[0],
        preferred_element_type=jnp.float32,
    )
    new_rounded = lax.optimization_barrier(new_weight.astype(jnp.bfloat16)).astype(jnp.float32)
    summed = summed + new_rounded[..., None] * value_new.astype(jnp.float32)[:, None, :]
    top_split = top.reshape(ROWS, 2, GR)
    total_split = total.reshape(ROWS, 2, GR)
    summed_split = summed.reshape(ROWS, 2, GR, HD)
    first_half = my_half == 0
    own_top = jnp.where(first_half, top_split[:, 0], top_split[:, 1])
    own_total = jnp.where(first_half, total_split[:, 0], total_split[:, 1])
    own_summed = jnp.where(first_half, summed_split[:, 0], summed_split[:, 1])
    give_top = jnp.where(first_half, top_split[:, 1], top_split[:, 0])
    give_total = jnp.where(first_half, total_split[:, 1], total_split[:, 0])
    give_summed = jnp.where(first_half, summed_split[:, 1], summed_split[:, 0])
    got_top, got_total, got_summed = from_partner((give_top, give_total, give_summed), "tp", 0)
    joint = jnp.maximum(own_top, got_top)
    factor_own = jnp.exp(own_top - joint)
    factor_got = jnp.exp(got_top - joint)
    numer = own_summed * factor_own[..., None] + got_summed * factor_got[..., None]
    denom = own_total * factor_own + got_total * factor_got
    attention = (numer / denom[..., None]).astype(jnp.bfloat16).reshape(ROWS, GR * HD)
    every_attn = lax.all_gather(attention[None], "tp", axis=0, tiled=True)
    head_ids = jnp.arange(KVH, dtype=jnp.int32)
    pair_heads = kv_assign[0::2]
    inverse = jnp.sum(
        head_ids[None, :] * (pair_heads[None, :] == head_ids[:, None]).astype(jnp.int32), axis=1
    )
    slot_ids = jnp.arange(QG, dtype=jnp.int32)
    rank_of_slot = 2 * inverse[slot_ids // 2] + slot_ids % 2
    attn_grid = every_attn.reshape(group_count, ROLL, ROWS, GR, HD)
    row_slot = lax.dynamic_index_in_dim(attn_grid, grid_row, 3, keepdims=False)
    chosen = jnp.take(row_slot, rank_of_slot, axis=1)
    out_part = jnp.einsum("gabe,cae->gbc", chosen, o_blocks[0], preferred_element_type=jnp.float32)
    placed = jnp.zeros((group_count, ROWS, D), jnp.float32)
    placed = lax.dynamic_update_slice_in_dim(placed, out_part, grid_col * col_width, 2)
    out_term = (
        placed.reshape(group_count, ROWS, ROLL, DS).transpose(0, 2, 1, 3).reshape(ranks * ROWS, DS)
    )
    my_cols = lax.psum_scatter(out_term, "tp", scatter_dimension=0, tiled=True)
    return my_cols.astype(jnp.bfloat16)[None]


def solution(mesh):
    return jax.shard_map(
        local,
        mesh=mesh,
        in_specs=(
            P(("groups", "tp"), None, None),
            P(),
            P("tp", None, None, None),
            P("tp", None, None, None),
            P(None, None, "tp"),
            P(),
            P(("groups", "tp"), None, None, None),
            P(("groups", "tp"), None, None, None),
            P(("groups", "tp"), None),
        ),
        out_specs=P(("groups", "tp"), None, None),
        check_vma=False,
    )
```

profile of v0, /device:TPU:0, one launch (start us, length us, event | category | flops | bytes accessed | tf_op | source)
XLA Modules:
  0.0 194.6 jit_solution(7086260716293882496)
XLA Ops:
  6.5 23.8 %all_gather.6 = bf16[16,8,512]{2,1,0:T(8,128)(2,1)S(1)} all-gather(bf16[1,8,512]{2,1,0:T(8,128)(2,1)} %param.9), channel_id=1, replica_groups=mesh['groups'=2,'tp'=16] {'tp'}, dimensions={0}, use_global_device_ids=true | all-gather | bytes 139264 | tf_op jit(solution)/shard_map/all_gather | solution.py:45
  30.3 0.2 multiply_reduce_fusion
  30.6 0.7 slice.41
  31.3 1.3 gather_fusion.1
  32.7 0.1 select_reduce_fusion.1
  32.8 0.7 gather_fusion
  33.5 0.1 broadcast_bitcast_fusion
  33.6 0.9 multiply_convert_fusion
  34.4 0.6 convolution_bitcast_fusion
  35.1 0.1 broadcast_in_dim.83
  35.2 0.1 broadcast_in_dim.84
  35.3 0.0 copy-start.2
  35.3 5.6 %fusion.17 = f32[16,8,128]{2,1,0:T(8,128)S(1)} fusion(bf16[1,16,128,2048]{3,2,1,0:T(8,128)(2,1)} %param.11, bf16[8,8192]{1,0:T(8,128)(2,1)S(1)} %multiply_convert_fusion, s32[]{:T(128)S(6)} %select_n.308), kind=kOutput, calls=%fused_computation.16 | convolution fusion | flops 67108864 | bytes 8486916 | tf_op jit(solution)/shard_map/rc,aec->rae/dot_general | solution.py:54
  41.0 0.6 gather_fusion.2
  41.5 0.1 broadcast_select_fusion
  41.7 0.6 gather_fusion.3
  42.2 0.1 bitcast_select_fusion
  42.3 0.8 pad_maximum_fusion
  43.1 0.0 reduce-scatter.3.cloned.1.call-update
  43.1 0.0 reduce-scatter.5.cloned.1.call-start
  43.3 0.1 iota_compare_fusion
  43.3 52.8 %reduce-scatter.3.cloned.1.call-done = f32[8,768]{1,0:T(8,128)} async-done(((f32[128,768]{1,0:T(8,128)}), f32[8,768]{1,0:T(8,128)}) %reduce-scatter.3.cloned.1.call-update) | async-done | bytes 24592 | tf_op jit(solution)/shard_map/reduce_scatter | solution.py:76
  96.1 0.7 convert.7
  96.9 0.0 collective-permute-start
  96.9 1.2 collective-permute-done
  98.1 0.1 fusion.41
  98.2 3.5 %select_reduce_fusion = (f32[8,8]{1,0:T(8,128)S(1)}, f32[8,8,2048]{2,1,0:T(8,128)S(1)}) fusion(pred[8,2048]{1,0:T(8,128)(4,1)S(1)} %iota_compare_fusion, bf16[1,8,2048,128]{3,2,1,0:T(8,128)(2,1)} %param.15, bf16[8,4,128]{2,1,0:T(4,128)(2,1)S(1)} %concatenate.18, bf16[8,4,128]{2,1,0:T(4,128)(2,1)S(1)} %concatenate.17, pred[]{:T(512)S(6)} %eq.39), kind=kOutput, calls=%fused_computation.20 | convolution fusion | flops 34021312 | bytes 4751617 | tf_op jit(solution)/shard_map/bhe,bte->bht/dot_general | solution.py:90
  101.7 0.1 copy.45
  101.8 0.2 collective-permute-start.1
  101.9 0.3 fusion.23
  102.2 0.1 copy.50
  102.3 0.3 collective-permute-start.3
  102.6 2.9 %fusion.20 = f32[8,8,128]{2,1,0:T(8,128)S(1)} fusion(bf16[1,8,2048,128]{3,2,1,0:T(8,128)(2,1)} %param.16, f32[8,8,2048]{2,1,0:T(8,128)S(1)} %get-tuple-element.17, f32[8,8]{1,0:T(8,128)S(1)} %fusion.43, pred[8,2048]{1,0:T(8,128)(4,1)S(1)} %iota_compare_fusion, f32[8,128]{1,0:T(8,128)S(1)} %get-tuple-element.8, f32[8,8]{1,0:T(8,128)S(1)} %convert_element_type.57), kind=kOutput, calls=%fused_computation.18 | convolution fusion | flops 33964032 | bytes 4772352 | tf_op jit(solution)/shard_map/bht,bte->bhe/dot_general | solution.py:103
  105.6 0.2 collective-permute-start.2
  105.8 0.0 collective-permute-done.1
  105.8 0.0 collective-permute-done.3
  105.8 0.1 copy.46
  105.9 0.1 copy.49
  106.0 0.1 copy.51
  106.1 0.8 collective-permute-done.2
  106.8 0.1 fusion.38
  106.9 19.8 %all_gather.7 = bf16[16,8,512]{2,1,0:T(8,128)(2,1)S(1)} all-gather(bf16[1,8,512]{2,1,0:T(8,128)(2,1)S(1)} %broadcast_in_dim_reshape.3), channel_id=1, replica_groups=mesh['groups'=2,'tp'=16] {'tp'}, dimensions={0}, use_global_device_ids=true | all-gather | bytes 139264 | tf_op jit(solution)/shard_map/all_gather | solution.py:128
  126.7 0.6 gather_fusion.4
  127.3 5.7 %fusion.14 = f32[1,8,8192]{2,1,0:T(8,128)S(1)} fusion(f32[1,8,8192]{2,1,0:T(8,128)S(1)} %broadcast_in_dim.78, s32[]{:T(128)S(6)} %select_n.308, bf16[2048,16,128]{2,1,0:T(8,128)(2,1)} %bitcast.146, bf16[16,8,128]{2,1,0:T(8,128)(2,1)S(1)} %gather_fusion.4, pred[16]{0:T(512)(128)(4,1)S(1)} %get-tuple-element.18), kind=kOutput, calls=%fused_computation.15 | convolution fusion | flops 67125248 | bytes 8487428 | tf_op jit(solution)/shard_map/gabe,cae->gbc/dot_general | solution.py:139
  132.9 0.7 copy-done.1
  133.6 0.0 reduce-scatter.5.cloned.1.call-update
  133.7 52.8 %reduce-scatter.5.cloned.1.call-done = f32[8,512]{1,0:T(8,128)} async-done(((f32[128,512]{1,0:T(8,128)}), f32[8,512]{1,0:T(8,128)}) %reduce-scatter.5.cloned.1.call-update) | async-done | bytes 16400 | tf_op jit(solution)/shard_map/reduce_scatter | solution.py:145
  186.4 1.3 convert_bitcast_fusion
  (33 shorter events, 0.3 us)
Async XLA Ops:
  6.5 27.9 %copy-start = (bf16[2,1024,512]{2,1,0:T(8,128)(2,1)S(1)}, bf16[2,1024,512]{2,1,0:T(8,128)(2,1)}, u32[]{:S(2)}) copy-start(bf16[2,1024,512]{2,1,0:T(8,128)(2,1)} %param.13) | copy-start | bytes 6291460
  6.5 89.6 %reduce-scatter.3.cloned.1.call-start = ((), (), s32[]{:S(2)}) async-start(), calls=%async_computation.2 | async-start | bytes 417792 | tf_op jit(solution)/shard_map/reduce_scatter | solution.py:76
  35.3 8.0 %copy-start.2 = (s32[1,8]{1,0:T(1,128)S(1)}, s32[1,8]{1,0:T(1,128)}, u32[]{:S(2)}) copy-start(s32[1,8]{1,0:T(1,128)} %param.17) | copy-start | bytes 100
  43.1 143.3 %reduce-scatter.5.cloned.1.call-start = ((), (), s32[]{:S(2)}) async-start(), calls=%async_computation.3 | async-start | bytes 278528 | tf_op jit(solution)/shard_map/reduce_scatter | solution.py:145
  96.9 1.2 collective-permute-start
  101.8 4.0 %collective-permute-start.1 = (f32[8,4]{0,1:T(4,128)S(1)}, f32[8,4]{0,1:T(4,128)S(1)}, u32[]{:S(2)}, u32[]{:S(2)}) collective-permute-start(f32[8,4]{0,1:T(4,128)S(1)} %select_bitcast_fusion.2), channel_id=1, source_target_pairs={{0,1},{1,0},{2,3},{3,2},{4,5},{5,4},{6,7},{7,6},{8,9},{9,8},{10,11... | collective-permute-start | bytes 392 | tf_op jit(solution)/shard_map/ppermute | solution.py:19
  102.3 3.5 %collective-permute-start.3 = (f32[8,4]{0,1:T(4,128)S(1)}, f32[8,4]{0,1:T(4,128)S(1)}, u32[]{:S(2)}, u32[]{:S(2)}) collective-permute-start(f32[8,4]{0,1:T(4,128)S(1)} %select_bitcast_fusion.1), channel_id=1, source_target_pairs={{0,1},{1,0},{2,3},{3,2},{4,5},{5,4},{6,7},{7,6},{8,9},{9,8},{10,11... | collective-permute-start | bytes 392 | tf_op jit(solution)/shard_map/ppermute | solution.py:19
  105.6 1.2 collective-permute-start.2
  132.9 0.7 copy-start.1
Sparse Core Ops, SparseCore 0:
  43.3 52.8 reduce-scatter.2
  133.8 52.5 reduce-scatter.4
where the time goes:
time: 195 us
  waiting for transfers between devices  107 us (55%)
  blocking collectives  43.5 us (22%)
  matrix products  18.4 us (9%)
  between operations  13.7 us (7%)
  local copies, waits for them, and re-layouts  5.86 us (3%)
  other arithmetic  4.78 us (2%)
    reduce_scatter x1, waiting for transfers between devices, local(): lax.psum_scatter(proj_term, 'tp', scatter_dimension=0, tiled=True)  52.8 us
    reduce_scatter x1, waiting for transfers between devices, local(): my_cols = lax.psum_scatter(out_term, 'tp', scatter_dimension=0, tiled=True)  52.8 us
    all_gather x1, blocking collectives, local(): every_rows = lax.all_gather(hidden_in, 'tp', axis=0, tiled=True)  23.8 us
    all_gather x1, blocking collectives, local(): every_attn = lax.all_gather(attention[None], 'tp', axis=0, tiled=True)  19.8 us
    dot_general x1, matrix products, local(): jnp.einsum('gabe,cae->gbc', chosen, o_blocks[0], preferred_element_type=j...  5.65 us
    dot_general x1, matrix products, local(): jnp.einsum('rc,aec->rae', col_rows, q_blocks[0], preferred_element_type=j...  5.65 us
  transfers between devices with their start and end apart: 6, of which 4 were waited for; matrix products, arithmetic and copies ran while one was open for 2% of the time, Pallas kernels for 0%

commit v1 on v0

--- a/solution.py
+++ b/solution.py
@@ -42,7 +42,25 @@
     dest_head = kv_assign[dest_rank]
     dest_group = 2 * dest_head + dest_rank % 2
     dest_copy = dest_ids // ROLL
-    every_rows = lax.all_gather(hidden_in, "tp", axis=0, tiled=True)
+    w_next = lax.axis_size("tp")
+    mixed_arr, heard, reached = (w_next, lax.axis_index("tp"), hidden_in.shape[0])
+    found = [j0 * mixed_arr if k0 == 0 else j0 for k0, j0 in enumerate(hidden_in.shape)]
+    a_next = parts_out = hidden_in
+    every_rows = lax.dynamic_update_slice_in_dim(
+        jnp.zeros(found, hidden_in.dtype), hidden_in, heard * reached, axis=0
+    )
+    for tick in [*range(1, mixed_arr // 2 + 1)]:
+        a_next = lax.ppermute(a_next, "tp", [(k0, (k0 + 1) % mixed_arr) for k0 in range(mixed_arr)])
+        every_rows = lax.dynamic_update_slice_in_dim(
+            every_rows, a_next, (heard - tick) % mixed_arr * reached, axis=0
+        )
+        if 2 * tick < mixed_arr:
+            parts_out = lax.ppermute(
+                parts_out, "tp", [(k0, (k0 - 1) % mixed_arr) for k0 in range(mixed_arr)]
+            )
+            every_rows = lax.dynamic_update_slice_in_dim(
+                every_rows, parts_out, (heard + tick) % mixed_arr * reached, axis=0
+            )
     rows_float = (
         every_rows.reshape(group_count, ROLL, ROWS, DS)
         .transpose(0, 2, 1, 3)

time: 195 us -> 218 us (1.12)
  starting transfers between devices: 0.8 us -> 32.8 us
  blocking collectives: 43.5 us -> 19.8 us
  waiting for transfers between devices: 107 us -> 122 us
    ppermute x0 -> x15, starting transfers between devices: none -> 32 us  [the longest x7 31.4 us: local(): lax.ppermute(parts_out, 'tp', [(k0, (k0 - 1) % mixed_arr) for k0 in range...]
    all_gather x1 -> x0, blocking collectives: 23.8 us -> none  [local(): every_rows = lax.all_gather(hidden_in, 'tp', axis=0, tiled=True)]
    ppermute x0 -> x15, waiting for transfers between devices: none -> 13.9 us  [the longest x8 13.7 us: local(): lax.ppermute(a_next, 'tp', [(k0, (k0 + 1) % mixed_arr) for k0 in range(mi...]
  transfers between devices with their start and end apart: 6 -> 21, of which waited for: 4 -> 11; matrix products, arithmetic and copies ran while one was open for 2% -> 3% of each run, Pallas kernels for 0% -> 0%
where the time goes in v1:
time: 218 us
  waiting for transfers between devices  122 us (56%)
  starting transfers between devices  32.8 us (15%)
  blocking collectives  19.8 us (9%)
  matrix products  18.4 us (8%)
  between operations  13.8 us (6%)
  local copies, waits for them, and re-layouts  6.6 us (3%)
  other arithmetic  4.79 us (2%)
    reduce_scatter x1, waiting for transfers between devices, local(): lax.psum_scatter(proj_term, 'tp', scatter_dimension=0, tiled=True)  53.3 us
    reduce_scatter x1, waiting for transfers between devices, local(): my_cols = lax.psum_scatter(out_term, 'tp', scatter_dimension=0, tiled=True)  52.7 us
    ppermute x7, starting transfers between devices, local(): lax.ppermute(parts_out, 'tp', [(k0, (k0 - 1) % mixed_arr) for k0 in range...  31.4 us
    all_gather x1, blocking collectives, local(): every_attn = lax.all_gather(attention[None], 'tp', axis=0, tiled=True)  19.8 us
    ppermute x8, waiting for transfers between devices, local(): lax.ppermute(a_next, 'tp', [(k0, (k0 + 1) % mixed_arr) for k0 in range(mi...  13.7 us
    dot_general x1, matrix products, local(): jnp.einsum('gabe,cae->gbc', chosen, o_blocks[0], preferred_element_type=j...  5.65 us
    dot_general x1, matrix products, local(): jnp.einsum('rc,aec->rae', col_rows, q_blocks[0], preferred_element_type=j...  5.65 us
  transfers between devices with their start and end apart: 21, of which 11 were waited for; matrix products, arithmetic and copies ran while one was open for 3% of the time, Pallas kernels for 0%

profile of v1, /device:TPU:0, one launch (start us, length us, event | category | flops | bytes accessed | tf_op | source)
XLA Modules:
  0.0 218.0 jit_solution(14329376513547302259)
XLA Ops:
  6.5 0.5 collective-permute-start
  7.0 5.0 %collective-permute-start.1 = (bf16[1,8,512]{2,1,0:T(8,128)(2,1)}, bf16[1,8,512]{2,1,0:T(8,128)(2,1)S(1)}, u32[]{:S(2)}, u32[]{:S(2)}) collective-permute-start(bf16[1,8,512]{2,1,0:T(8,128)(2,1)} %param.9), channel_id=1, source_target_pairs={{0,15},{1,0},{2,1},{3,2},{4,3},{5,4},{6,5},{7,6},{8,7},{9,8},{10,9... | collective-permute-start | bytes 24584 | tf_op jit(solution)/shard_map/ppermute | solution.py:58
  12.0 0.7 slice.41
  12.7 1.3 gather_fusion.1
  14.1 0.1 select_reduce_fusion.1
  14.2 0.7 gather_fusion
  15.0 0.7 bitcast_dynamic-update-slice_fusion.15
  15.8 0.1 broadcast_in_dim.85
  16.1 4.4 %collective-permute-start.3 = (bf16[1,8,512]{2,1,0:T(8,128)(2,1)S(1)}, bf16[1,8,512]{2,1,0:T(8,128)(2,1)S(1)}, u32[]{:S(2)}, u32[]{:S(2)}) collective-permute-start(bf16[1,8,512]{2,1,0:T(8,128)(2,1)S(1)} %collective-permute-done.1), channel_id=1, source_target_pairs={{0,15},{1,0},{2,1},{3,2},{4,3},{5,4},{6,5},{7,6},{8,7},{9,8},{10,9... | collective-permute-start | bytes 24584 | tf_op jit(solution)/shard_map/ppermute | solution.py:58
  20.5 1.4 collective-permute-done.2
  21.9 4.4 %collective-permute-start.5 = (bf16[1,8,512]{2,1,0:T(8,128)(2,1)S(1)}, bf16[1,8,512]{2,1,0:T(8,128)(2,1)S(1)}, u32[]{:S(2)}, u32[]{:S(2)}) collective-permute-start(bf16[1,8,512]{2,1,0:T(8,128)(2,1)S(1)} %collective-permute-done.3), channel_id=1, source_target_pairs={{0,15},{1,0},{2,1},{3,2},{4,3},{5,4},{6,5},{7,6},{8,7},{9,8},{10,9... | collective-permute-start | bytes 24584 | tf_op jit(solution)/shard_map/ppermute | solution.py:58
  26.3 1.3 collective-permute-done.4
  27.7 4.4 %collective-permute-start.7 = (bf16[1,8,512]{2,1,0:T(8,128)(2,1)S(1)}, bf16[1,8,512]{2,1,0:T(8,128)(2,1)S(1)}, u32[]{:S(2)}, u32[]{:S(2)}) collective-permute-start(bf16[1,8,512]{2,1,0:T(8,128)(2,1)S(1)} %collective-permute-done.5), channel_id=1, source_target_pairs={{0,15},{1,0},{2,1},{3,2},{4,3},{5,4},{6,5},{7,6},{8,7},{9,8},{10,9... | collective-permute-start | bytes 24584 | tf_op jit(solution)/shard_map/ppermute | solution.py:58
  32.1 1.3 collective-permute-done.6
  33.4 4.4 %collective-permute-start.9 = (bf16[1,8,512]{2,1,0:T(8,128)(2,1)S(1)}, bf16[1,8,512]{2,1,0:T(8,128)(2,1)S(1)}, u32[]{:S(2)}, u32[]{:S(2)}) collective-permute-start(bf16[1,8,512]{2,1,0:T(8,128)(2,1)S(1)} %collective-permute-done.7), channel_id=1, source_target_pairs={{0,15},{1,0},{2,1},{3,2},{4,3},{5,4},{6,5},{7,6},{8,7},{9,8},{10,9... | collective-permute-start | bytes 24584 | tf_op jit(solution)/shard_map/ppermute | solution.py:58
  37.8 1.3 collective-permute-done.8
  39.2 4.4 %collective-permute-start.11 = (bf16[1,8,512]{2,1,0:T(8,128)(2,1)S(1)}, bf16[1,8,512]{2,1,0:T(8,128)(2,1)S(1)}, u32[]{:S(2)}, u32[]{:S(2)}) collective-permute-start(bf16[1,8,512]{2,1,0:T(8,128)(2,1)S(1)} %collective-permute-done.9), channel_id=1, source_target_pairs={{0,15},{1,0},{2,1},{3,2},{4,3},{5,4},{6,5},{7,6},{8,7},{9,8},{10,9... | collective-permute-start | bytes 24584 | tf_op jit(solution)/shard_map/ppermute | solution.py:58
  43.6 1.3 collective-permute-done.10
  45.0 4.4 %collective-permute-start.13 = (bf16[1,8,512]{2,1,0:T(8,128)(2,1)S(1)}, bf16[1,8,512]{2,1,0:T(8,128)(2,1)S(1)}, u32[]{:S(2)}, u32[]{:S(2)}) collective-permute-start(bf16[1,8,512]{2,1,0:T(8,128)(2,1)S(1)} %collective-permute-done.11), channel_id=1, source_target_pairs={{0,15},{1,0},{2,1},{3,2},{4,3},{5,4},{6,5},{7,6},{8,7},{9,8},{10,9... | collective-permute-start | bytes 24584 | tf_op jit(solution)/shard_map/ppermute | solution.py:58
  49.4 1.3 collective-permute-done.12
  50.8 5.7 %collective-permute-done.14 = bf16[1,8,512]{2,1,0:T(8,128)(2,1)S(1)} collective-permute-done((bf16[1,8,512]{2,1,0:T(8,128)(2,1)S(1)}, bf16[1,8,512]{2,1,0:T(8,128)(2,1)S(1)}, u32[]{:S(2)}, u32[]{:S(2)}) %collective-permute-start.14) | collective-permute-done | bytes 8224 | tf_op jit(solution)/shard_map/ppermute | solution.py:53
  56.5 0.2 multiply_reduce_fusion
  56.7 0.9 multiply_convert_fusion
  57.6 0.6 convolution_bitcast_fusion
  58.3 5.7 %fusion.17 = f32[16,8,128]{2,1,0:T(8,128)S(1)} fusion(bf16[1,16,128,2048]{3,2,1,0:T(8,128)(2,1)} %param.11, bf16[8,8192]{1,0:T(8,128)(2,1)S(1)} %multiply_convert_fusion, s32[]{:T(128)S(6)} %select_n.447), kind=kOutput, calls=%fused_computation.16 | convolution fusion | flops 67108864 | bytes 8486916 | tf_op jit(solution)/shard_map/rc,aec->rae/dot_general | solution.py:72
  63.9 0.6 gather_fusion.2
  64.5 0.1 broadcast_select_fusion
  64.6 0.6 gather_fusion.3
  65.2 0.1 bitcast_select_fusion
  65.3 0.8 pad_maximum_fusion
  66.3 53.3 %reduce-scatter.3.cloned.1.call-done = f32[8,768]{1,0:T(8,128)} async-done(((f32[128,768]{1,0:T(8,128)}), f32[8,768]{1,0:T(8,128)}) %reduce-scatter.3.cloned.1.call-update) | async-done | bytes 24592 | tf_op jit(solution)/shard_map/reduce_scatter | solution.py:94
  119.6 0.7 convert.6
  120.3 1.2 collective-permute-done.15
  121.5 0.1 fusion.43
  121.6 3.5 %select_reduce_fusion = (f32[8,8]{1,0:T(8,128)S(1)}, f32[8,8,2048]{2,1,0:T(8,128)S(1)}) fusion(pred[8,2048]{1,0:T(8,128)(4,1)S(1)} %iota_compare_fusion, bf16[1,8,2048,128]{3,2,1,0:T(8,128)(2,1)} %param.15, bf16[8,4,128]{2,1,0:T(4,128)(2,1)S(1)} %concatenate.18, bf16[8,4,128]{2,1,0:T(4,128)(2,1)S(1)} %concatenate.17, pred[]{:T(512)S(6)} %eq.54), kind=kOutput, calls=%fused_computation.20 | convolution fusion | flops 34021312 | bytes 4751617 | tf_op jit(solution)/shard_map/bhe,bte->bht/dot_general | solution.py:108
  125.2 0.2 collective-permute-start.16
  125.4 0.3 fusion.23
  125.7 0.3 collective-permute-start.18
  126.1 2.9 %fusion.20 = f32[8,8,128]{2,1,0:T(8,128)S(1)} fusion(bf16[1,8,2048,128]{3,2,1,0:T(8,128)(2,1)} %param.16, f32[8,8,2048]{2,1,0:T(8,128)S(1)} %get-tuple-element.17, f32[8,8]{1,0:T(8,128)S(1)} %fusion.45, pred[8,2048]{1,0:T(8,128)(4,1)S(1)} %iota_compare_fusion, f32[8,128]{1,0:T(8,128)S(1)} %get-tuple-element.8, f32[8,8]{1,0:T(8,128)S(1)} %convert_element_type.52), kind=kOutput, calls=%fused_computation.18 | convolution fusion | flops 33964032 | bytes 4772352 | tf_op jit(solution)/shard_map/bht,bte->bhe/dot_general | solution.py:121
  129.0 0.2 collective-permute-start.17
  129.5 0.8 collective-permute-done.17
  130.2 0.1 fusion.38
  130.3 19.8 %all_gather.3 = bf16[16,8,512]{2,1,0:T(8,128)(2,1)S(1)} all-gather(bf16[1,8,512]{2,1,0:T(8,128)(2,1)S(1)} %broadcast_in_dim_reshape.3), channel_id=1, replica_groups=mesh['groups'=2,'tp'=16] {'tp'}, dimensions={0}, use_global_device_ids=true | all-gather | bytes 139264 | tf_op jit(solution)/shard_map/all_gather | solution.py:146
  150.1 0.6 gather_fusion.4
  150.7 5.7 %fusion.14 = f32[1,8,8192]{2,1,0:T(8,128)S(1)} fusion(f32[1,8,8192]{2,1,0:T(8,128)S(1)} %broadcast_in_dim.79, s32[]{:T(128)S(6)} %select_n.447, bf16[2048,16,128]{2,1,0:T(8,128)(2,1)} %bitcast.176, bf16[16,8,128]{2,1,0:T(8,128)(2,1)S(1)} %gather_fusion.4, pred[16]{0:T(512)(128)(4,1)S(1)} %get-tuple-element.18), kind=kOutput, calls=%fused_computation.15 | convolution fusion | flops 67125248 | bytes 8487428 | tf_op jit(solution)/shard_map/gabe,cae->gbc/dot_general | solution.py:157
  156.4 0.7 copy-done.1
  157.1 52.7 %reduce-scatter.5.cloned.1.call-done = f32[8,512]{1,0:T(8,128)} async-done(((f32[128,512]{1,0:T(8,128)}), f32[8,512]{1,0:T(8,128)}) %reduce-scatter.5.cloned.1.call-update) | async-done | bytes 16400 | tf_op jit(solution)/shard_map/reduce_scatter | solution.py:163
  209.8 1.3 convert_bitcast_fusion
  (79 shorter events, 1.3 us)
Async XLA Ops:
  6.5 51.0 %copy-start = (bf16[2,1024,512]{2,1,0:T(8,128)(2,1)S(1)}, bf16[2,1024,512]{2,1,0:T(8,128)(2,1)}, u32[]{:S(2)}) copy-start(bf16[2,1024,512]{2,1,0:T(8,128)(2,1)} %param.13) | copy-start | bytes 6291460
  6.5 113.0 %reduce-scatter.3.cloned.1.call-start = ((), (), s32[]{:S(2)}) async-start(), calls=%async_computation.2 | async-start | bytes 417792 | tf_op jit(solution)/shard_map/reduce_scatter | solution.py:94
  6.5 9.4 %collective-permute-start = (bf16[1,8,512]{2,1,0:T(8,128)(2,1)}, bf16[1,8,512]{2,1,0:T(8,128)(2,1)S(1)}, u32[]{:S(2)}, u32[]{:S(2)}) collective-permute-start(bf16[1,8,512]{2,1,0:T(8,128)(2,1)} %param.9), channel_id=1, source_target_pairs={{0,1},{1,2},{2,3},{3,4},{4,5},{5,6},{6,7},{7,8},{8,9},{9,10},{10,1... | collective-permute-start | bytes 24584 | tf_op jit(solution)/shard_map/ppermute | solution.py:53
  7.0 9.1 %collective-permute-start.1 = (bf16[1,8,512]{2,1,0:T(8,128)(2,1)}, bf16[1,8,512]{2,1,0:T(8,128)(2,1)S(1)}, u32[]{:S(2)}, u32[]{:S(2)}) collective-permute-start(bf16[1,8,512]{2,1,0:T(8,128)(2,1)} %param.9), channel_id=1, source_target_pairs={{0,15},{1,0},{2,1},{3,2},{4,3},{5,4},{6,5},{7,6},{8,7},{9,8},{10,9... | collective-permute-start | bytes 24584 | tf_op jit(solution)/shard_map/ppermute | solution.py:58
  16.0 5.9 %collective-permute-start.2 = (bf16[1,8,512]{2,1,0:T(8,128)(2,1)S(1)}, bf16[1,8,512]{2,1,0:T(8,128)(2,1)S(1)}, u32[]{:S(2)}, u32[]{:S(2)}) collective-permute-start(bf16[1,8,512]{2,1,0:T(8,128)(2,1)S(1)} %collective-permute-done), channel_id=1, source_target_pairs={{0,1},{1,2},{2,3},{3,4},{4,5},{5,6},{6,7},{7,8},{8,9},{9,10},{10,1... | collective-permute-start | bytes 24584 | tf_op jit(solution)/shard_map/ppermute | solution.py:53
  16.1 5.8 %collective-permute-start.3 = (bf16[1,8,512]{2,1,0:T(8,128)(2,1)S(1)}, bf16[1,8,512]{2,1,0:T(8,128)(2,1)S(1)}, u32[]{:S(2)}, u32[]{:S(2)}) collective-permute-start(bf16[1,8,512]{2,1,0:T(8,128)(2,1)S(1)} %collective-permute-done.1), channel_id=1, source_target_pairs={{0,15},{1,0},{2,1},{3,2},{4,3},{5,4},{6,5},{7,6},{8,7},{9,8},{10,9... | collective-permute-start | bytes 24584 | tf_op jit(solution)/shard_map/ppermute | solution.py:58
  21.8 5.8 %collective-permute-start.4 = (bf16[1,8,512]{2,1,0:T(8,128)(2,1)S(1)}, bf16[1,8,512]{2,1,0:T(8,128)(2,1)S(1)}, u32[]{:S(2)}, u32[]{:S(2)}) collective-permute-start(bf16[1,8,512]{2,1,0:T(8,128)(2,1)S(1)} %collective-permute-done.2), channel_id=1, source_target_pairs={{0,1},{1,2},{2,3},{3,4},{4,5},{5,6},{6,7},{7,8},{8,9},{9,10},{10,1... | collective-permute-start | bytes 24584 | tf_op jit(solution)/shard_map/ppermute | solution.py:53
  21.9 5.8 %collective-permute-start.5 = (bf16[1,8,512]{2,1,0:T(8,128)(2,1)S(1)}, bf16[1,8,512]{2,1,0:T(8,128)(2,1)S(1)}, u32[]{:S(2)}, u32[]{:S(2)}) collective-permute-start(bf16[1,8,512]{2,1,0:T(8,128)(2,1)S(1)} %collective-permute-done.3), channel_id=1, source_target_pairs={{0,15},{1,0},{2,1},{3,2},{4,3},{5,4},{6,5},{7,6},{8,7},{9,8},{10,9... | collective-permute-start | bytes 24584 | tf_op jit(solution)/shard_map/ppermute | solution.py:58
  27.6 5.8 %collective-permute-start.6 = (bf16[1,8,512]{2,1,0:T(8,128)(2,1)S(1)}, bf16[1,8,512]{2,1,0:T(8,128)(2,1)S(1)}, u32[]{:S(2)}, u32[]{:S(2)}) collective-permute-start(bf16[1,8,512]{2,1,0:T(8,128)(2,1)S(1)} %collective-permute-done.4), channel_id=1, source_target_pairs={{0,1},{1,2},{2,3},{3,4},{4,5},{5,6},{6,7},{7,8},{8,9},{9,10},{10,1... | collective-permute-start | bytes 24584 | tf_op jit(solution)/shard_map/ppermute | solution.py:53
  27.7 5.8 %collective-permute-start.7 = (bf16[1,8,512]{2,1,0:T(8,128)(2,1)S(1)}, bf16[1,8,512]{2,1,0:T(8,128)(2,1)S(1)}, u32[]{:S(2)}, u32[]{:S(2)}) collective-permute-start(bf16[1,8,512]{2,1,0:T(8,128)(2,1)S(1)} %collective-permute-done.5), channel_id=1, source_target_pairs={{0,15},{1,0},{2,1},{3,2},{4,3},{5,4},{6,5},{7,6},{8,7},{9,8},{10,9... | collective-permute-start | bytes 24584 | tf_op jit(solution)/shard_map/ppermute | solution.py:58
  33.4 5.8 %collective-permute-start.8 = (bf16[1,8,512]{2,1,0:T(8,128)(2,1)S(1)}, bf16[1,8,512]{2,1,0:T(8,128)(2,1)S(1)}, u32[]{:S(2)}, u32[]{:S(2)}) collective-permute-start(bf16[1,8,512]{2,1,0:T(8,128)(2,1)S(1)} %collective-permute-done.6), channel_id=1, source_target_pairs={{0,1},{1,2},{2,3},{3,4},{4,5},{5,6},{6,7},{7,8},{8,9},{9,10},{10,1... | collective-permute-start | bytes 24584 | tf_op jit(solution)/shard_map/ppermute | solution.py:53
  33.4 5.8 %collective-permute-start.9 = (bf16[1,8,512]{2,1,0:T(8,128)(2,1)S(1)}, bf16[1,8,512]{2,1,0:T(8,128)(2,1)S(1)}, u32[]{:S(2)}, u32[]{:S(2)}) collective-permute-start(bf16[1,8,512]{2,1,0:T(8,128)(2,1)S(1)} %collective-permute-done.7), channel_id=1, source_target_pairs={{0,15},{1,0},{2,1},{3,2},{4,3},{5,4},{6,5},{7,6},{8,7},{9,8},{10,9... | collective-permute-start | bytes 24584 | tf_op jit(solution)/shard_map/ppermute | solution.py:58
  39.2 5.8 %collective-permute-start.10 = (bf16[1,8,512]{2,1,0:T(8,128)(2,1)S(1)}, bf16[1,8,512]{2,1,0:T(8,128)(2,1)S(1)}, u32[]{:S(2)}, u32[]{:S(2)}) collective-permute-start(bf16[1,8,512]{2,1,0:T(8,128)(2,1)S(1)} %collective-permute-done.8), channel_id=1, source_target_pairs={{0,1},{1,2},{2,3},{3,4},{4,5},{5,6},{6,7},{7,8},{8,9},{9,10},{10,1... | collective-permute-start | bytes 24584 | tf_op jit(solution)/shard_map/ppermute | solution.py:53
  39.2 5.8 %collective-permute-start.11 = (bf16[1,8,512]{2,1,0:T(8,128)(2,1)S(1)}, bf16[1,8,512]{2,1,0:T(8,128)(2,1)S(1)}, u32[]{:S(2)}, u32[]{:S(2)}) collective-permute-start(bf16[1,8,512]{2,1,0:T(8,128)(2,1)S(1)} %collective-permute-done.9), channel_id=1, source_target_pairs={{0,15},{1,0},{2,1},{3,2},{4,3},{5,4},{6,5},{7,6},{8,7},{9,8},{10,9... | collective-permute-start | bytes 24584 | tf_op jit(solution)/shard_map/ppermute | solution.py:58
  44.9 5.8 %collective-permute-start.12 = (bf16[1,8,512]{2,1,0:T(8,128)(2,1)S(1)}, bf16[1,8,512]{2,1,0:T(8,128)(2,1)S(1)}, u32[]{:S(2)}, u32[]{:S(2)}) collective-permute-start(bf16[1,8,512]{2,1,0:T(8,128)(2,1)S(1)} %collective-permute-done.10), channel_id=1, source_target_pairs={{0,1},{1,2},{2,3},{3,4},{4,5},{5,6},{6,7},{7,8},{8,9},{9,10},{10,1... | collective-permute-start | bytes 24584 | tf_op jit(solution)/shard_map/ppermute | solution.py:53
  45.0 5.8 %collective-permute-start.13 = (bf16[1,8,512]{2,1,0:T(8,128)(2,1)S(1)}, bf16[1,8,512]{2,1,0:T(8,128)(2,1)S(1)}, u32[]{:S(2)}, u32[]{:S(2)}) collective-permute-start(bf16[1,8,512]{2,1,0:T(8,128)(2,1)S(1)} %collective-permute-done.11), channel_id=1, source_target_pairs={{0,15},{1,0},{2,1},{3,2},{4,3},{5,4},{6,5},{7,6},{8,7},{9,8},{10,9... | collective-permute-start | bytes 24584 | tf_op jit(solution)/shard_map/ppermute | solution.py:58
  50.7 5.8 %collective-permute-start.14 = (bf16[1,8,512]{2,1,0:T(8,128)(2,1)S(1)}, bf16[1,8,512]{2,1,0:T(8,128)(2,1)S(1)}, u32[]{:S(2)}, u32[]{:S(2)}) collective-permute-start(bf16[1,8,512]{2,1,0:T(8,128)(2,1)S(1)} %collective-permute-done.12), channel_id=1, source_target_pairs={{0,1},{1,2},{2,3},{3,4},{4,5},{5,6},{6,7},{7,8},{8,9},{9,10},{10,1... | collective-permute-start | bytes 24584 | tf_op jit(solution)/shard_map/ppermute | solution.py:53
  58.2 8.0 %copy-start.2 = (s32[1,8]{1,0:T(1,128)S(1)}, s32[1,8]{1,0:T(1,128)}, u32[]{:S(2)}) copy-start(s32[1,8]{1,0:T(1,128)} %param.17) | copy-start | bytes 100
  66.1 143.8 %reduce-scatter.5.cloned.1.call-start = ((), (), s32[]{:S(2)}) async-start(), calls=%async_computation.3 | async-start | bytes 278528 | tf_op jit(solution)/shard_map/reduce_scatter | solution.py:163
  120.3 1.2 collective-permute-start.15
  125.2 4.0 %collective-permute-start.16 = (f32[8,4]{0,1:T(4,128)S(1)}, f32[8,4]{0,1:T(4,128)S(1)}, u32[]{:S(2)}, u32[]{:S(2)}) collective-permute-start(f32[8,4]{0,1:T(4,128)S(1)} %select_bitcast_fusion.2), channel_id=1, source_target_pairs={{0,1},{1,0},{2,3},{3,2},{4,5},{5,4},{6,7},{7,6},{8,9},{9,8},{10,11... | collective-permute-start | bytes 392 | tf_op jit(solution)/shard_map/ppermute | solution.py:19
  125.7 3.5 %collective-permute-start.18 = (f32[8,4]{0,1:T(4,128)S(1)}, f32[8,4]{0,1:T(4,128)S(1)}, u32[]{:S(2)}, u32[]{:S(2)}) collective-permute-start(f32[8,4]{0,1:T(4,128)S(1)} %select_bitcast_fusion.1), channel_id=1, source_target_pairs={{0,1},{1,0},{2,3},{3,2},{4,5},{5,4},{6,7},{7,6},{8,9},{9,8},{10,11... | collective-permute-start | bytes 392 | tf_op jit(solution)/shard_map/ppermute | solution.py:19
  129.0 1.2 collective-permute-start.17
  156.4 0.7 copy-start.1
Sparse Core Ops, SparseCore 0:
  66.2 53.3 reduce-scatter.2
  157.2 52.5 reduce-scatter.4
